TPU v7x, 32 devices: a whole 2x2x4 slice. The times are simulated.
32 devices in a mesh: dp: 8 (over y, x, core), tensor: 4 (over z).
Axes of the slice: x: 2, y: 2, z: 4, core: 2. Of those that a mesh axis runs over, the one named last changes fastest.
Arguments:
- hidden_in: bfloat16 [16, 1024, 2048], P('dp', 'tensor'), may hold values from -6 to 6
- keep_slot: int32 [16], P('dp'), may hold values 0 or 1
- out_grad: bfloat16 [16, 1024, 2048], P('dp', 'tensor'), may hold values from -8 to 8
- ln1_gain: bfloat16 [2048], replicated, may hold values from 0.5 to 1.5
- ln1_bias: bfloat16 [2048], replicated, may hold values from -1.25 to 1.25
- ln2_gain: bfloat16 [2048], replicated, may hold values from 0.5 to 1.5
- ln2_bias: bfloat16 [2048], replicated, may hold values from -1.25 to 1.25
- qkv_weight: bfloat16 [2048, 6144], P(None, 'tensor'), may hold values from -0.125 to 0.125
- qkv_bias: bfloat16 [8, 768], P('tensor'), may hold values from -0.625 to 0.625
- dense_weight: bfloat16 [2048, 2048], P('tensor'), may hold values from -0.75 to 0.75
- dense_bias: bfloat16 [2048], replicated, may hold values from -1.25 to 1.25
- fc1_weight: bfloat16 [2048, 8192], P(None, 'tensor'), may hold values from -0.125 to 0.125
- fc1_bias: bfloat16 [8192], P('tensor'), may hold values from -1.25 to 1.25
- fc2_weight: bfloat16 [8192, 2048], P('tensor'), may hold values from -0.0625 to 0.0625
- fc2_bias: bfloat16 [2048], replicated, may hold values from -1.25 to 1.25
Outputs:
- block_out: bfloat16 [16, 1024, 2048], P('dp', 'tensor')
- hidden_grad: float32 [16, 1024, 2048], P('dp', 'tensor')
- ln1_gain_grad: float32 [2048], P(('dp', 'tensor'))
- ln1_bias_grad: float32 [2048], P(('dp', 'tensor'))
- ln2_gain_grad: float32 [2048], P(('dp', 'tensor'))
- ln2_bias_grad: float32 [2048], P(('dp', 'tensor'))
- qkv_weight_grad: float32 [2048, 6144], P('dp', 'tensor')
- qkv_bias_grad: float32 [8, 768], P('tensor', 'dp')
- dense_weight_grad: float32 [2048, 2048], P('tensor', 'dp')
- dense_bias_grad: float32 [2048], P(('dp', 'tensor'))
- fc1_weight_grad: float32 [2048, 8192], P('dp', 'tensor')
- fc1_bias_grad: float32 [4, 2048], P('tensor', 'dp')
- fc2_weight_grad: float32 [8192, 2048], P('tensor', 'dp')
- fc2_bias_grad: float32 [2048], P(('dp', 'tensor'))
All inputs are finite; a program needn't handle non-finite values. No bound on the sum of `keep_slot` on one device may be relied on, other than what follows from the above.
Results may differ from a plain program's by a relative error of at most 0.0092.
Values may be sent and summed in bfloat16 or wider, within the bound.
No kernel may reach another device: no remote copies, remote signals or barrier semaphores. Data moves between devices by JAX's collectives and lax.ppermute only.
A program may use at most 320 MiB of HBM per device.

v0:
```python
import math
import jax
import jax.numpy as jnp
from jax import lax
from jax.sharding import PartitionSpec as P

ROT = 64
layer_eps = 1e-05
rope_base = 10000.0
mask_fill = -1e30
block_rows = 512


def rope_tables(length, rot_dims):
    half = rot_dims // 2
    freqs = jnp.exp(-jnp.log(rope_base) * (2.0 * jnp.arange(half, dtype=jnp.float32) / rot_dims))
    angles = jnp.arange(length, dtype=jnp.float32)[:, None] * freqs[None, :]
    return (jnp.cos(angles), jnp.sin(angles))


def rotate(field, cosine, sine, rot_dims, sign):
    half = rot_dims // 2
    first = field[..., :half]
    second = field[..., half:rot_dims]
    rest = field[..., rot_dims:]
    cos_b = cosine[:, None, :]
    sin_b = sign * sine[:, None, :]
    return jnp.concatenate(
        [first * cos_b - second * sin_b, second * cos_b + first * sin_b, rest], axis=-1
    )


def gelu_exact(field):
    return jax.nn.gelu(field, approximate=False)


def contract_rows(left, right):
    return lax.dot_general(
        left, right, (((0,), (0,)), ((), ())), preferred_element_type=jnp.float32
    )


def contract_cols(left, right):
    return lax.dot_general(
        left, right, (((1,), (1,)), ((), ())), preferred_element_type=jnp.float32
    )


def local(
    hidden_in,
    keep_slot,
    out_grad,
    ln1_gain,
    ln1_bias,
    ln2_gain,
    ln2_bias,
    qkv_weight,
    qkv_bias,
    dense_weight,
    dense_bias,
    fc1_weight,
    fc1_bias,
    fc2_weight,
    fc2_bias,
):
    slot_count, own_len, width = hidden_in.shape
    seq_len = own_len * lax.axis_size("tensor")
    head_local, three_hd = qkv_bias.shape
    head_dim = three_hd // 3
    scale = 1.0 / math.sqrt(head_dim)
    start_row = lax.axis_index("tensor") * own_len
    inputs_all, grads_all = (
        lax.all_gather(hidden_in, "tensor", axis=1, tiled=True),
        lax.all_gather(out_grad, "tensor", axis=1, tiled=True),
    )
    cosine, sine = rope_tables(seq_len, ROT)
    blk = min(block_rows, seq_len)
    n_blocks = seq_len // blk
    key_pos = jnp.arange(seq_len)
    starts = jnp.arange(n_blocks) * blk
    qkv_acc = jnp.zeros(qkv_weight.shape, jnp.float32)
    dense_acc = jnp.zeros(dense_weight.shape, jnp.float32)
    up_acc = jnp.zeros(fc1_weight.shape, jnp.float32)
    down_acc = jnp.zeros(fc2_weight.shape, jnp.float32)
    qkv_bias_acc = jnp.zeros((head_local * three_hd,), jnp.float32)
    up_bias_acc = jnp.zeros(fc1_bias.shape, jnp.float32)
    gain_one_acc = jnp.zeros((width,), jnp.float32)
    shift_one_acc = jnp.zeros((width,), jnp.float32)
    gain_two_acc = jnp.zeros((width,), jnp.float32)
    shift_two_acc = jnp.zeros((width,), jnp.float32)
    out_bias_acc = jnp.zeros((width,), jnp.float32)
    out_rows = []
    grad_rows_out = []
    for slot_idx in range(slot_count):
        keep = keep_slot[slot_idx].astype(jnp.float32)
        rows_full = inputs_all[slot_idx].astype(jnp.float32)
        centred = rows_full - jnp.mean(rows_full, axis=-1, keepdims=True)
        inv_std = lax.rsqrt(jnp.mean(centred * centred, axis=-1, keepdims=True) + layer_eps)
        normed = centred * inv_std
        normed_one = (normed * ln1_gain + ln1_bias).astype(jnp.bfloat16)
        normed_two = (normed * ln2_gain + ln2_bias).astype(jnp.bfloat16)
        joined = jnp.dot(
            normed_one, qkv_weight, preferred_element_type=jnp.float32
        ) + qkv_bias.reshape(-1)
        joined = joined.reshape(seq_len, head_local, 3, head_dim)
        query_rot = rotate(joined[:, :, 0], cosine, sine, ROT, 1.0).astype(jnp.bfloat16)
        key_rot = rotate(joined[:, :, 1], cosine, sine, ROT, 1.0).astype(jnp.bfloat16)
        value_rows = joined[:, :, 2].astype(jnp.bfloat16)
        query_blocks = query_rot.reshape(n_blocks, blk, head_local, head_dim)

        def block_scores(query_blk, blk_start):
            scores = (
                jnp.einsum("bhd,khd->hbk", query_blk, key_rot, preferred_element_type=jnp.float32)
                * scale
            )
            allowed = key_pos[None, :] <= (blk_start + jnp.arange(blk))[:, None]
            return jnp.where(allowed[None], scores, mask_fill)

        def attend(items):
            query_blk, blk_start = items
            scores = block_scores(query_blk, blk_start)
            top = jnp.max(scores, axis=-1, keepdims=True)
            weights = jnp.exp(scores - top)
            total = jnp.sum(weights, axis=-1, keepdims=True)
            probs = weights / total
            mixed = jnp.einsum(
                "hbk,khd->bhd",
                probs.astype(jnp.bfloat16),
                value_rows,
                preferred_element_type=jnp.float32,
            )
            return (mixed.astype(jnp.bfloat16), (top + jnp.log(total))[..., 0])

        attn_blocks, log_total = lax.map(attend, (query_blocks, starts))
        attn_flat = attn_blocks.reshape(seq_len, head_local * head_dim)
        pre_act = jnp.dot(normed_two, fc1_weight, preferred_element_type=jnp.float32) + fc1_bias
        act_val, act_back = jax.vjp(gelu_exact, pre_act)
        act_low = act_val.astype(jnp.bfloat16)
        partial_out = jnp.dot(
            attn_flat, dense_weight, preferred_element_type=jnp.float32
        ) + jnp.dot(act_low, fc2_weight, preferred_element_type=jnp.float32)
        summed = lax.psum(partial_out, "tensor")
        branch_own = lax.dynamic_slice_in_dim(summed, start_row, own_len, 0)
        branch_own = branch_own + dense_bias + fc2_bias
        own_in = hidden_in[slot_idx].astype(jnp.float32)
        out_rows.append((own_in + keep * branch_own).astype(jnp.bfloat16))
        branch_grad = grads_all[slot_idx] * keep_slot[slot_idx].astype(jnp.bfloat16)
        own_cot = out_grad[slot_idx].astype(jnp.float32)
        out_bias_acc = out_bias_acc + jnp.sum(own_cot * keep, axis=0)
        down_acc = down_acc + contract_rows(act_low, branch_grad)
        dense_acc = dense_acc + contract_rows(attn_flat, branch_grad)
        act_grad = contract_cols(branch_grad, fc2_weight)
        pre_grad = act_back(act_grad)[0].astype(jnp.bfloat16)
        up_bias_acc = up_bias_acc + jnp.sum(pre_grad.astype(jnp.float32), axis=0)
        up_acc = up_acc + contract_rows(normed_two, pre_grad)
        normed_two_grad = contract_cols(pre_grad, fc1_weight)
        mixed_grad = contract_cols(branch_grad, dense_weight).astype(jnp.bfloat16)
        grad_blocks = mixed_grad.reshape(n_blocks, blk, head_local, head_dim)

        def attend_back(carry, items):
            key_acc, value_acc = carry
            query_blk, grad_blk, lse_blk, blk_start = items
            scores = block_scores(query_blk, blk_start)
            probs = jnp.exp(scores - lse_blk[..., None])
            probs_low = probs.astype(jnp.bfloat16)
            prob_grad = jnp.einsum(
                "bhd,khd->hbk", grad_blk, value_rows, preferred_element_type=jnp.float32
            )
            inner = jnp.sum(probs * prob_grad, axis=-1, keepdims=True)
            score_grad = (probs * (prob_grad - inner)).astype(jnp.bfloat16)
            query_grad = (
                jnp.einsum("hbk,khd->bhd", score_grad, key_rot, preferred_element_type=jnp.float32)
                * scale
            )
            key_acc = (
                key_acc
                + jnp.einsum(
                    "hbk,bhd->khd", score_grad, query_blk, preferred_element_type=jnp.float32
                )
                * scale
            )
            value_acc = value_acc + jnp.einsum(
                "hbk,bhd->khd", probs_low, grad_blk, preferred_element_type=jnp.float32
            )
            return ((key_acc, value_acc), query_grad)

        empty = jnp.zeros((seq_len, head_local, head_dim), jnp.float32)
        (key_grad, value_grad), query_grad = lax.scan(
            attend_back, (empty, empty), (query_blocks, grad_blocks, log_total, starts)
        )
        query_grad = rotate(
            query_grad.reshape(seq_len, head_local, head_dim), cosine, sine, ROT, -1.0
        )
        key_grad = rotate(key_grad, cosine, sine, ROT, -1.0)
        joined_grad = (
            jnp.stack([query_grad, key_grad, value_grad], axis=2)
            .reshape(seq_len, head_local * three_hd)
            .astype(jnp.bfloat16)
        )
        qkv_bias_acc = qkv_bias_acc + jnp.sum(joined_grad.astype(jnp.float32), axis=0)
        qkv_acc = qkv_acc + contract_rows(normed_one, joined_grad)
        normed_one_grad = contract_cols(joined_grad, qkv_weight)
        gain_one_acc = gain_one_acc + jnp.sum(normed_one_grad * normed, axis=0)
        shift_one_acc = shift_one_acc + jnp.sum(normed_one_grad, axis=0)
        gain_two_acc = gain_two_acc + jnp.sum(normed_two_grad * normed, axis=0)
        shift_two_acc = shift_two_acc + jnp.sum(normed_two_grad, axis=0)
        normed_grad = normed_one_grad * ln1_gain + normed_two_grad * ln2_gain
        grad_summed = lax.psum(normed_grad.astype(jnp.bfloat16), "tensor").astype(jnp.float32)
        own_grad = lax.dynamic_slice_in_dim(grad_summed, start_row, own_len, 0)
        own_normed = lax.dynamic_slice_in_dim(normed, start_row, own_len, 0)
        own_inv = lax.dynamic_slice_in_dim(inv_std, start_row, own_len, 0)
        back_rows = own_inv * (
            own_grad
            - jnp.mean(own_grad, axis=-1, keepdims=True)
            - own_normed * jnp.mean(own_grad * own_normed, axis=-1, keepdims=True)
        )
        grad_rows_out.append(own_cot + back_rows)
    weight_parts = (
        lax.psum_scatter(qkv_acc, "dp", scatter_dimension=0, tiled=True),
        lax.psum_scatter(dense_acc, "dp", scatter_dimension=1, tiled=True),
        lax.psum_scatter(up_acc, "dp", scatter_dimension=0, tiled=True),
        lax.psum_scatter(down_acc, "dp", scatter_dimension=1, tiled=True),
        lax.psum_scatter(
            qkv_bias_acc.reshape(head_local, three_hd), "dp", scatter_dimension=1, tiled=True
        ),
        lax.psum_scatter(up_bias_acc.reshape(1, -1), "dp", scatter_dimension=1, tiled=True),
    )
    small_parts = lax.psum_scatter(
        jnp.stack([gain_one_acc, shift_one_acc, gain_two_acc, shift_two_acc, out_bias_acc]),
        ("dp", "tensor"),
        scatter_dimension=1,
        tiled=True,
    )
    block_out = jnp.stack(out_rows)
    hidden_grad = jnp.stack(grad_rows_out)
    return (
        block_out,
        hidden_grad,
        small_parts[0],
        small_parts[1],
        small_parts[2],
        small_parts[3],
        weight_parts[0],
        weight_parts[4],
        weight_parts[1],
        small_parts[4],
        weight_parts[2],
        weight_parts[5],
        weight_parts[3],
        small_parts[4],
    )


def solution(mesh):
    in_specs = (
        P("dp", "tensor", None),
        P("dp"),
        P("dp", "tensor", None),
        P(),
        P(),
        P(),
        P(),
        P(None, "tensor"),
        P("tensor", None),
        P("tensor", None),
        P(),
        P(None, "tensor"),
        P("tensor"),
        P("tensor", None),
        P(),
    )
    out_specs = (
        P("dp", "tensor", None),
        P("dp", "tensor", None),
        P(("dp", "tensor")),
        P(("dp", "tensor")),
        P(("dp", "tensor")),
        P(("dp", "tensor")),
        P("dp", "tensor"),
        P("tensor", "dp"),
        P("tensor", "dp"),
        P(("dp", "tensor")),
        P("dp", "tensor"),
        P("tensor", "dp"),
        P("tensor", "dp"),
        P(("dp", "tensor")),
    )
    return jax.shard_map(local, mesh=mesh, in_specs=in_specs, out_specs=out_specs, check_vma=False)
```

profile of v0, /device:TPU:0, one launch (start us, length us, event | category | flops | bytes accessed | tf_op | source)
XLA Modules:
  0.0 2166.4 jit_solution(5631583935324290304)
XLA Ops:
  13.9 148.1 %all-gather.3.cloned.1.call-done = bf16[2,1024,2048]{2,1,0:T(8,128)(2,1)} async-done(((bf16[2,256,2048]{2,1,0:T(8,128)(2,1)}), bf16[2,1024,2048]{2,1,0:T(8,128)(2,1)}) %all-gather.3.cloned.1.call-update) | async-done | bytes 8388624 | tf_op jit(solution)/shard_map/all_gather | solution.py:73
  162.0 4.2 convert_reduce_fusion.1
  171.5 8.9 convolution_add_fusion.4
  180.4 6.6 copy.95
  187.7 12.4 convolution_add_fusion.3
  200.0 6.6 copy.103
  219.6 3.2 concatenate.49
  230.4 3.1 pad_maximum_fusion.4
  233.5 2.8 fusion.152
  236.9 17.1 while.57
  254.0 57.4 %all-gather.5.cloned.1.call-done = bf16[2,1024,2048]{2,1,0:T(8,128)(2,1)} async-done(((bf16[2,256,2048]{2,1,0:T(8,128)(2,1)}), bf16[2,1024,2048]{2,1,0:T(8,128)(2,1)}) %all-gather.5.cloned.1.call-update) | async-done | bytes 8388624 | tf_op jit(solution)/shard_map/all_gather | solution.py:74
  311.4 5.5 convolution_convert_fusion
  319.1 41.9 %while.59 = (s32[]{:T(128)}, f32[1024,2,256]{0,2,1:T(8,128)}, f32[1024,2,256]{0,2,1:T(8,128)}, f32[2,512,2,256]{3,1,0,2:T(8,128)}, bf16[2,512,2,256]{3,1,2,0:T(8...) while((s32[]{:T(128)}, f32[1024,2,256]{0,2,1:T(8,128)}, ...), condition=%wide.region_22.23_spmd.clone, body=%wide.region_20.22_spmd.clone.sunk | while | flops 2703490560 | bytes 112231744 | solution.py:188
  328.9 4.0 bitcast_add_fusion.10
  336.2 2.9 bitcast_add_fusion.11
  348.6 4.7 bitcast_add_fusion.10
  356.5 4.5 bitcast_add_fusion.11
  361.0 3.4 fusion.165
  371.4 3.2 concatenate.44
  374.7 3.6 copy.99
  380.5 3.5 pad_maximum_fusion.2
  385.5 15.8 while.56
  401.3 5.5 convolution_convert_fusion.1
  408.9 82.9 %while.58 = (s32[]{:T(128)}, f32[1024,2,256]{0,2,1:T(8,128)}, f32[1024,2,256]{0,2,1:T(8,128)}, f32[2,512,2,256]{1,0,3,2:T(2,128)}, bf16[2,512,2,256]{3,1,2,0:T(8...) while((s32[]{:T(128)}, f32[1024,2,256]{0,2,1:T(8,128)}, ...), condition=%wide.region_16.17_spmd.clone, body=%wide.region_14.16_spmd.clone.sunk | while | flops 2703490560 | bytes 112231848 | solution.py:188
  419.2 3.6 copy.207
  422.7 19.6 dynamic_update_slice.42
  442.3 4.0 bitcast_add_fusion.8
  446.3 2.9 bitcast_add_fusion.9
  459.5 3.6 copy.207
  463.1 19.6 dynamic_update_slice.42
  482.6 4.6 bitcast_add_fusion.8
  487.3 4.5 bitcast_add_fusion.9
  491.8 4.1 reshape.564
  529.6 4.7 copy.129
  534.3 11.9 fusion.170
  546.3 10.9 fusion.172
  557.3 11.8 fusion.162
  569.2 50.6 %multiply_convert_fusion.3 = (bf16[1024,2048]{1,0:T(8,128)(2,1)}, f32[1024,2048]{1,0:T(8,128)}, bf16[1024,2048]{1,0:T(8,128)(2,1)}, f32[1024,2048]{1,0:T(8,128)}, f32[1024,2048]{1,0:T(8,128)}) fusion(f32[2048]{0:T(1024)S(1)} %copy-done.52, f32[1024,2048]{1,0:T(8,128)} %fusion.162, bf16[2048,2048]{1,0:T(8,128)(2,1)S(1)} %bitcast.409, ...), kind=kOutput, calls=%fused_computation.149 | convolution fusion | flops 8879341568 | bytes 54558720 | tf_op jit(solution)/shard_map/dot_general | solution.py:136
  619.7 19.0 convert_reduce_fusion.3
  638.7 14.8 fusion.171
  653.5 20.4 convert_reduce_fusion.2
  673.9 29.7 %multiply_reduce_fusion.2 = (f32[2048]{0:T(1024)S(1)}, f32[2048]{0:T(1024)S(1)}, f32[2048]{0:T(1024)S(1)}, f32[2048]{0:T(1024)S(1)}, f32[2048]{0:T(1024)S(1)}, /...) fusion(f32[1024]{0:T(1024)S(1)} %copy-done.55, ...), kind=kOutput, calls=%fused_computation.126 | convolution fusion | flops 8644444160 | bytes 71401472 | tf_op jit(solution)/shard_map/dot_general | solution.py:44
  706.0 15.5 fusion.168
  721.6 14.7 fusion.169
  740.5 9.4 convolution_add_fusion.6
  749.9 242.9 %all-reduce.7.cloned.1.call-done = (bf16[1024,2048]{1,0:T(8,128)(2,1)}, bf16[1024,2048]{1,0:T(8,128)(2,1)}) async-done(((bf16[1024,2048]{1,0:T(8,128)(2,1)}, bf16[1024,2048]{1,0:T(8,128)(2,1)}), (bf16[1024,2048]{1,0:T(8,128)(2,1)}, bf16[1024,2048]{1,0:T(8,128)(2,1)})) %all-reduce.7.cloned.1.call-update) | async-done | bytes 8388624 | tf_op jit(solution)/shard_map/psum | solution.py:208
  997.8 5.1 fusion.125
  1004.9 9.1 convolution_add_fusion.5
  1014.0 4.9 fusion.136
  1018.9 6.5 convolution_add_fusion.7
  1026.1 14.5 fusion.102
  1040.7 16.0 convolution_add_fusion
  1057.4 15.9 fusion.160
  1073.3 17.9 convolution_add_fusion.2
  1091.5 15.4 fusion.134
  1106.9 17.1 convolution_add_fusion.1
  1127.8 4.7 pad_maximum_fusion
  1132.5 74.2 %reduce-scatter.22.cloned.1.call-done = f32[64,5]{1,0:T(8,128)} async-done(((f32[2048,5]{1,0:T(8,128)}), f32[64,5]{1,0:T(8,128)}) %reduce-scatter.22.cloned.1.call-update) | async-done | bytes 1296
  1210.3 557.9 %all-reduce.5.cloned.1.call-done = (f32[1024,2048]{1,0:T(8,128)}, f32[1024,2048]{1,0:T(8,128)}) async-done(((f32[1024,2048]{1,0:T(8,128)}, f32[1024,2048]{1,0:T(8,128)}), (f32[1024,2048]{1,0:T(8,128)}, f32[1024,2048]{1,0:T(8,128)})) %all-reduce.5.cloned.1.call-update) | async-done | bytes 16777232 | tf_op jit(solution)/shard_map/psum | solution.py:142
  1768.2 3.7 fusion.150
  1773.5 48.7 %reduce-scatter.16.cloned.1.call-done = f32[512,256]{1,0:T(8,128)} async-done(((f32[512,2048]{1,0:T(8,128)}), f32[512,256]{1,0:T(8,128)}) %reduce-scatter.16.cloned.1.call-update) | async-done | bytes 524304 | tf_op jit(solution)/shard_map/reduce_scatter | solution.py:220
  1822.2 96.4 %reduce-scatter.14.cloned.1.call-done = f32[256,1536]{1,0:T(8,128)} async-done(((f32[2048,1536]{1,0:T(8,128)}), f32[256,1536]{1,0:T(8,128)}) %reduce-scatter.14.cloned.1.call-update) | async-done | bytes 1572880 | tf_op jit(solution)/shard_map/reduce_scatter | solution.py:219
  1918.6 120.2 %reduce-scatter.18.cloned.1.call-done = f32[256,2048]{1,0:T(8,128)} async-done(((f32[2048,2048]{1,0:T(8,128)}), f32[256,2048]{1,0:T(8,128)}) %reduce-scatter.18.cloned.1.call-update) | async-done | bytes 2097168 | tf_op jit(solution)/shard_map/reduce_scatter | solution.py:221
  2038.8 120.2 %reduce-scatter.20.cloned.1.call-done = f32[2048,256]{1,0:T(8,128)} async-done(((f32[2048,2048]{1,0:T(8,128)}), f32[2048,256]{1,0:T(8,128)}) %reduce-scatter.20.cloned.1.call-update) | async-done | bytes 2097168 | tf_op jit(solution)/shard_map/reduce_scatter | solution.py:222
  (385 shorter events, 182.0 us)
Async XLA Ops:
  7.2 304.2 %copy-start = (bf16[512,2048]{1,0:T(8,128)(2,1)S(1)}, bf16[512,2048]{1,0:T(8,128)(2,1)}, u32[]{:S(2)}) copy-start(bf16[512,2048]{1,0:T(8,128)(2,1)} %param.32) | copy-start | bytes 6291460
  7.2 4.8 copy-start.60
  7.2 5.4 copy-start.61
  7.3 6.0 copy-start.62
  7.3 154.7 %all-gather.3.cloned.1.call-start = ((), (), s32[]{:S(2)}) async-start(), calls=%async_computation.7 | async-start | bytes 10485760 | tf_op jit(solution)/shard_map/all_gather | solution.py:73
  8.0 303.4 %all-gather.5.cloned.1.call-start = ((), (), s32[]{:S(2)}) async-start(), calls=%async_computation.8 | async-start | bytes 10485760 | tf_op jit(solution)/shard_map/all_gather | solution.py:74
  8.8 984.1 %all-reduce.7.cloned.1.call-start = ((), (), s32[]{:S(2)}) async-start(), calls=%async_computation.17 | async-start | bytes 16777216 | tf_op jit(solution)/shard_map/psum | solution.py:208
  8.9 178.1 %copy-start.48 = (f32[2048]{0:T(1024)}, f32[2048]{0:T(1024)S(1)}, u32[]{:S(2)}) copy-start(f32[2048]{0:T(1024)S(1)} %convert_element_type.255) | copy-start | bytes 24580
  8.9 178.1 %copy-start.50 = (f32[2048]{0:T(1024)}, f32[2048]{0:T(1024)S(1)}, u32[]{:S(2)}) copy-start(f32[2048]{0:T(1024)S(1)} %convert_element_type.256) | copy-start | bytes 24580
  10.2 203.0 %copy-start.33 = (f32[1024,32]{0,1:T(8,128)}, f32[1024,32]{0,1:T(8,128)S(1)}, u32[]{:S(2)}) copy-start(f32[1024,32]{0,1:T(8,128)S(1)} %get-tuple-element.592) | copy-start | bytes 393220
  162.0 5.9 copy-start.13
  166.3 4.4 copy-start.43
  166.3 20.8 copy-start.40
  206.6 4.8 slice-start.2
  206.6 4.8 slice-start.3
  254.0 63.0 %copy-start.22 = (bf16[2,512,2,256]{3,2,1,0:T(2,128)(2,1)}, bf16[2,512,2,256]{3,2,1,0:T(2,128)(2,1)S(1)}, u32[]{:S(2)}) copy-start(bf16[2,512,2,256]{3,2,1,0:T(2,128)(2,1)S(1)} %get-tuple-element.219) | copy-start | bytes 3145732
  321.7 4.9 copy-start.3
  328.9 7.3 copy-start.4
  341.4 4.9 copy-start.3
  348.6 4.7 copy-start.6
  348.6 4.7 copy-start.17
  348.6 7.9 copy-start.4
  361.0 4.8 copy-start.27
  408.9 4.1 copy-start.12
  410.8 4.0 copy-start.1
  449.2 4.1 copy-start.12
  482.6 4.7 copy-start.2
  482.6 4.7 copy-start.8
  482.6 4.7 copy-start.10
  491.8 5.7 copy-start.24
  495.9 9.2 copy-start.34
  507.8 10.9 copy-start.37
  511.7 8.4 copy-start.35
  511.7 8.4 copy-start.36
  534.3 11.9 copy-start.25
  534.3 22.9 %slice-start = ((s8[8388608]{0:T(1024)(128)(4,1)}), s8[4194304]{0:T(1024)(128)(4,1)S(1)}, s32[]{:S(2)}) async-start(s8[8388608]{0:T(1024)(128)(4,1)} %bitcast.368), calls=%async_computation.18 | async-start | bytes 8388608
  534.3 22.9 %slice-start.4 = ((s8[8388608]{0:T(1024)(128)(4,1)}), s8[4194304]{0:T(1024)(128)(4,1)S(1)}, s32[]{:S(2)}) async-start(s8[8388608]{0:T(1024)(128)(4,1)} %bitcast.408), calls=%async_computation.22 | async-start | bytes 8388608
  546.2 11.0 slice-start.1
  546.2 11.0 slice-start.5
  546.2 11.0 copy-start.41
  546.3 11.0 copy-start.45
  546.3 11.0 copy-start.46
  546.3 11.0 copy-start.54
  557.3 11.9 copy-start.44
  557.3 11.9 copy-start.52
  557.3 11.9 copy-start.57
  638.7 14.8 copy-start.71
  653.5 20.4 copy-start.42
  653.5 20.4 copy-start.49
  653.5 20.4 copy-start.55
  703.6 421.1 %reduce-scatter.24.cloned.1.call-start = ((), (), s32[]{:S(2)}) async-start(), calls=%async_computation.14 | async-start | bytes 442368
  721.5 404.7 %reduce-scatter.26.cloned.1.call-start = ((), (), s32[]{:S(2)}) async-start(), calls=%async_computation.15 | async-start | bytes 1179648
  721.6 17.3 copy-start.23
  740.5 466.3 %reduce-scatter.22.cloned.1.call-start = ((), (), s32[]{:S(2)}) async-start(), calls=%async_computation.13 | async-start | bytes 1081344
  992.8 5.0 copy-start.16
  1004.4 763.8 %all-reduce.5.cloned.1.call-start = ((), (), s32[]{:S(2)}) async-start(), calls=%async_computation.16 | async-start | bytes 33554432 | tf_op jit(solution)/shard_map/psum | solution.py:142
  1014.0 808.2 %reduce-scatter.16.cloned.1.call-start = ((), (), s32[]{:S(2)}) async-start(), calls=%async_computation.10 | async-start | bytes 4718592 | tf_op jit(solution)/shard_map/reduce_scatter | solution.py:220
  1025.5 893.1 %reduce-scatter.14.cloned.1.call-start = ((), (), s32[]{:S(2)}) async-start(), calls=%async_computation.9 | async-start | bytes 14155776 | tf_op jit(solution)/shard_map/reduce_scatter | solution.py:219
  1026.1 14.5 copy-start.26
  1056.7 982.0 %reduce-scatter.18.cloned.1.call-start = ((), (), s32[]{:S(2)}) async-start(), calls=%async_computation.11 | async-start | bytes 18874368 | tf_op jit(solution)/shard_map/reduce_scatter | solution.py:221
  1057.4 15.9 copy-start.70
  1091.2 1067.7 %reduce-scatter.20.cloned.1.call-start = ((), (), s32[]{:S(2)}) async-start(), calls=%async_computation.12 | async-start | bytes 18874368 | tf_op jit(solution)/shard_map/reduce_scatter | solution.py:222
  1091.5 15.4 copy-start.69
  1207.9 951.0 %copy-start.67 = (f32[1,64]{1,0:T(1,128)}, f32[1,64]{1,0:T(1,128)S(1)}, u32[]{:S(2)}) copy-start(f32[1,64]{1,0:T(1,128)S(1)} %copy.159) | copy-start | bytes 772
  (41 other events, 101.1 us)
Sparse Core Ops, SparseCore 0:
  9.6 152.3 all-gather.2
  163.6 147.7 all-gather.4
  703.8 289.0 all-reduce.6
  995.7 32.8 reduce-scatter.23
  1031.7 35.9 reduce-scatter.25
  1069.8 136.9 reduce-scatter.21
  1209.4 558.7 all-reduce.4
  1772.1 49.9 reduce-scatter.15
  1826.2 92.3 reduce-scatter.13
  1922.6 116.1 reduce-scatter.17
  2042.9 115.9 reduce-scatter.19
where the time goes:
time: 2180 us; the launch traced here: 2170 us
  waiting for transfers between devices  1470 us (67%)
  matrix products  433 us (20%)
  local copies, waits for them, and re-layouts  175 us (8%)
  other arithmetic  70 us (3%)
    psum x1, waiting for transfers between devices, local(): summed = lax.psum(partial_out, 'tensor')  558 us
    psum x1, waiting for transfers between devices, local(): lax.psum(normed_grad.astype(jnp.bfloat16), 'tensor').astype(jnp.float32)  243 us
    all_gather x1, waiting for transfers between devices, local(): lax.all_gather(hidden_in, 'tensor', axis=1, tiled=True)  148 us
    reduce_scatter x1, waiting for transfers between devices, local(): lax.psum_scatter(up_acc, 'dp', scatter_dimension=0, tiled=True)  120 us
    reduce_scatter x1, waiting for transfers between devices, local(): lax.psum_scatter(down_acc, 'dp', scatter_dimension=1, tiled=True)  120 us
    dot_general x8, matrix products, contract_cols(): lax.dot_general(left, right, (((1,), (1,)), ((), ())), preferred_element_...  118 us
    dot_general x8, matrix products, contract_rows(): lax.dot_general(left, right, (((0,), (0,)), ((), ())), preferred_element_...  108 us
    reduce_scatter x1, waiting for transfers between devices, local(): lax.psum_scatter(qkv_acc, 'dp', scatter_dimension=0, tiled=True)  96.4 us
  transfers between devices with their start and end apart: 11, of which 9 were waited for; matrix products, arithmetic and copies ran while one was open for 13% of the time, Pallas kernels for 0%

commit v1 on v0

--- a/solution.py
+++ b/solution.py
@@ -9,6 +9,37 @@
 rope_base = 10000.0
 mask_fill = -1e30
 block_rows = 512
+
+
+def node_expand(block_here, dimension_no):
+    block_here = jnp.moveaxis(block_here, 0, dimension_no)
+    v_now = block_here.shape
+    return block_here.reshape(
+        *v_now[:dimension_no],
+        v_now[dimension_no] * v_now[dimension_no + 1],
+        *v_now[dimension_no + 2 :]
+    )
+
+
+def expand_indices(x_local, mesh_dim):
+    latest = x_local[None]
+    count_all = jax.lax.axis_size(mesh_dim)
+    for idx in range(count_all.bit_length() - 1):
+        now = 1 << idx
+        panels = []
+        for m in range(count_all):
+            panels.append((m, m ^ now))
+        met_up = jax.lax.ppermute(latest, mesh_dim, perm=panels)
+        new = jnp.stack([latest, met_up])
+        f_next = jax.lax.axis_index(mesh_dim)
+        vec_out = f_next >> idx & 1
+        latest = jnp.where(vec_out == 0, new, new[::-1]).reshape(-1, *x_local.shape)
+    return latest
+
+
+def boxes_fit(patch, payload, along_dim):
+    prior = expand_indices(patch, payload)
+    return node_expand(prior, along_dim)
 
 
 def rope_tables(length, rot_dims):
@@ -70,7 +101,7 @@
     scale = 1.0 / math.sqrt(head_dim)
     start_row = lax.axis_index("tensor") * own_len
     inputs_all, grads_all = (
-        lax.all_gather(hidden_in, "tensor", axis=1, tiled=True),
+        boxes_fit(hidden_in, "tensor", 1),
         lax.all_gather(out_grad, "tensor", axis=1, tiled=True),
     )
     cosine, sine = rope_tables(seq_len, ROT)

time: 2180 us -> 2390 us (1.096)
  waiting for transfers between devices: 1470 us -> 1630 us
  other arithmetic: 70 us -> 117 us
  matrix products: 433 us -> 407 us
    ppermute x0 -> x2, waiting for transfers between devices: none -> 357 us  [expand_indices(): met_up = jax.lax.ppermute(latest, mesh_dim, perm=panels)]
    all_gather x1 -> x0, waiting for transfers between devices: 148 us -> none  [local(): lax.all_gather(hidden_in, 'tensor', axis=1, tiled=True)]
    all_gather x1, waiting for transfers between devices: 57.4 us -> 0.01 us  [local(): lax.all_gather(out_grad, 'tensor', axis=1, tiled=True)]
    unnamed x14 -> x13, waiting for transfers between devices: 75.8 us -> 79.5 us
  transfers between devices with their start and end apart: 11 -> 12, of which waited for: 9 -> 9; matrix products, arithmetic and copies ran while one was open for 13% -> 18% of each run, Pallas kernels for 0% -> 0%
where the time goes in v1:
time: 2390 us; the launch traced here: 2380 us
  waiting for transfers between devices  1630 us (68%)
  matrix products  407 us (17%)
  local copies, waits for them, and re-layouts  194 us (8%)
  other arithmetic  117 us (5%)
    psum x1, waiting for transfers between devices, local(): summed = lax.psum(partial_out, 'tensor')  558 us
    ppermute x2, waiting for transfers between devices, expand_indices(): met_up = jax.lax.ppermute(latest, mesh_dim, perm=panels)  357 us
    psum x1, waiting for transfers between devices, local(): lax.psum(normed_grad.astype(jnp.bfloat16), 'tensor').astype(jnp.float32)  253 us
    reduce_scatter x1, waiting for transfers between devices, local(): lax.psum_scatter(up_acc, 'dp', scatter_dimension=0, tiled=True)  120 us
    reduce_scatter x1, waiting for transfers between devices, local(): lax.psum_scatter(down_acc, 'dp', scatter_dimension=1, tiled=True)  120 us
    dot_general x8, matrix products, contract_cols(): lax.dot_general(left, right, (((1,), (1,)), ((), ())), preferred_element_...  115 us
    dot_general x8, matrix products, contract_rows(): lax.dot_general(left, right, (((0,), (0,)), ((), ())), preferred_element_...  98.5 us
    reduce_scatter x1, waiting for transfers between devices, local(): lax.psum_scatter(qkv_acc, 'dp', scatter_dimension=0, tiled=True)  96.4 us
  transfers between devices with their start and end apart: 12, of which 9 were waited for; matrix products, arithmetic and copies ran while one was open for 18% of the time, Pallas kernels for 0%

profile of v1, /device:TPU:0, one launch (start us, length us, event | category | flops | bytes accessed | tf_op | source)
XLA Modules:
  0.0 2377.6 jit_solution(2246316840383940598)
XLA Ops:
  10.4 45.9 %collective-permute-done = bf16[1,2,256,2048]{3,2,1,0:T(8,128)(2,1)} collective-permute-done((bf16[1,2,256,2048]{3,2,1,0:T(8,128)(2,1)}, bf16[1,2,256,2048]{3,2,1,0:T(8,128)(2,1)}, u32[]{:S(2)}, u32[]{:S(2)}) %collective-permute-start) | collective-permute-done | bytes 2097184 | tf_op jit(solution)/shard_map/ppermute | solution.py:32
  59.0 4.9 fusion.88
  70.7 311.0 %collective-permute-done.1 = bf16[2,2,256,2048]{3,2,1,0:T(8,128)(2,1)} collective-permute-done((bf16[2,2,256,2048]{3,2,1,0:T(8,128)(2,1)}, bf16[2,2,256,2048]{3,2,1,0:T(8,128)(2,1)}, u32[]{:S(2)}, u32[]{:S(2)}) %collective-permute-start.1) | collective-permute-done | bytes 4194336 | tf_op jit(solution)/shard_map/ppermute | solution.py:32
  381.7 7.5 pad_maximum_fusion
  389.2 14.2 reverse_select_fusion
  403.4 8.3 copy_bitcast_fusion.6
  411.8 4.7 convert_reduce_fusion.3
  421.4 9.1 add_convert_fusion.8
  430.5 10.5 convolution_add_fusion.4
  441.0 6.6 copy.98
  447.6 5.0 slice_bitcast_fusion.2
  455.3 10.5 convolution_add_fusion.3
  465.8 6.6 copy.106
  492.1 3.6 copy.102
  502.9 15.6 while.56
  536.7 3.6 pad_maximum_fusion.6
  541.8 16.1 while.57
  557.9 12.6 fusion.135
  573.8 48.6 %multiply_convert_fusion.3 = (bf16[1024,2048]{1,0:T(8,128)(2,1)}, f32[1024,2048]{1,0:T(8,128)}, bf16[1024,2048]{1,0:T(8,128)(2,1)}, f32[1024,2048]{1,0:T(8,128)}, f32[1024,2048]{1,0:T(8,128)}) fusion(f32[2048]{0:T(1024)S(1)} %copy-done.74, f32[1024,2048]{1,0:T(8,128)S(1)} %fusion.135, bf16[1024,2048]{1,0:T(8,128)(2,1)S(1)} %copy-done.28, ...), kind=kOutput, calls=%fused_computation.137 | convolution fusion | flops 8866758656 | bytes 54534144 | tf_op jit(solution)/shard_map/dot_general | solution.py:167
  622.5 4.5 convolution_convert_fusion
  628.1 40.3 %while.59 = (s32[]{:T(128)}, f32[1024,2,256]{0,2,1:T(8,128)}, f32[1024,2,256]{0,2,1:T(8,128)}, f32[2,512,2,256]{3,1,0,2:T(8,128)}, bf16[2,512,2,256]{3,1,2,0:T(8...) while((s32[]{:T(128)}, f32[1024,2,256]{0,2,1:T(8,128)}, ...), condition=%wide.region_22.23_spmd.clone, body=%wide.region_20.22_spmd.clone.sunk | while | flops 2703490560 | bytes 116426080 | solution.py:219
  637.1 4.0 bitcast_add_fusion.10
  655.9 4.7 bitcast_add_fusion.10
  663.9 4.5 bitcast_add_fusion.11
  673.1 5.6 convolution_convert_fusion.1
  680.9 83.7 %while.58 = (s32[]{:T(128)}, f32[1024,2,256]{0,2,1:T(8,128)}, f32[1024,2,256]{0,2,1:T(8,128)}, f32[2,512,2,256]{1,0,3,2:T(2,128)}, bf16[2,512,2,256]{3,1,2,0:T(8...) while((s32[]{:T(128)}, f32[1024,2,256]{0,2,1:T(8,128)}, ...), condition=%wide.region_16.17_spmd.clone, body=%wide.region_14.16_spmd.clone.sunk | while | flops 2703490560 | bytes 112231848 | solution.py:219
  691.4 3.6 copy.217
  695.0 19.6 dynamic_update_slice.42
  714.7 4.1 bitcast_add_fusion.8
  732.0 3.6 copy.217
  735.6 19.6 dynamic_update_slice.42
  755.3 4.7 bitcast_add_fusion.8
  760.0 4.5 bitcast_add_fusion.9
  764.5 4.1 reshape.619
  802.4 4.7 copy.132
  807.0 12.1 fusion.137
  819.1 10.9 fusion.139
  830.0 19.2 convert_reduce_fusion.1
  849.2 14.9 fusion.138
  864.1 20.3 convert_reduce_fusion
  884.4 27.5 %multiply_reduce_fusion.2 = (f32[2048]{0:T(1024)S(1)}, f32[2048]{0:T(1024)S(1)}, f32[2048]{0:T(1024)S(1)}, f32[2048]{0:T(1024)S(1)}, f32[2048]{0:T(1024)S(1)}, /...) fusion(f32[1024]{0:T(1024)S(1)} %bitcast.422, ...), kind=kOutput, calls=%fused_computation.113 | convolution fusion | flops 8644444160 | bytes 63012864 | tf_op jit(solution)/shard_map/dot_general | solution.py:75
  914.8 12.8 fusion.134
  927.7 5.6 convolution_add_fusion.6
  933.3 13.4 fusion.136
  950.7 253.2 %all-reduce.7.cloned.1.call-done = (bf16[1024,2048]{1,0:T(8,128)(2,1)}, bf16[1024,2048]{1,0:T(8,128)(2,1)}) async-done(((bf16[1024,2048]{1,0:T(8,128)(2,1)}, bf16[1024,2048]{1,0:T(8,128)(2,1)}), (bf16[1024,2048]{1,0:T(8,128)(2,1)}, bf16[1024,2048]{1,0:T(8,128)(2,1)})) %all-reduce.7.cloned.1.call-update) | async-done | bytes 8388624 | tf_op jit(solution)/shard_map/psum | solution.py:239
  1209.0 5.1 fusion.92
  1215.8 9.0 convolution_add_fusion.5
  1224.9 4.9 fusion.103
  1229.8 6.6 convolution_add_fusion.7
  1237.1 5.6 add_convert_fusion
  1242.7 9.6 fusion.140
  1252.3 13.2 convolution_add_fusion
  1265.7 15.5 fusion.141
  1281.3 16.0 convolution_add_fusion.2
  1297.6 15.5 fusion.101
  1313.1 17.3 convolution_add_fusion.1
  1334.0 4.7 pad_maximum_fusion.2
  1338.8 79.3 %reduce-scatter.22.cloned.1.call-done = f32[64,5]{1,0:T(8,128)} async-done(((f32[2048,5]{1,0:T(8,128)}), f32[64,5]{1,0:T(8,128)}) %reduce-scatter.22.cloned.1.call-update) | async-done | bytes 1296
  1421.6 557.7 %all-reduce.5.cloned.1.call-done = (f32[1024,2048]{1,0:T(8,128)}, f32[1024,2048]{1,0:T(8,128)}) async-done(((f32[1024,2048]{1,0:T(8,128)}, f32[1024,2048]{1,0:T(8,128)}), (f32[1024,2048]{1,0:T(8,128)}, f32[1024,2048]{1,0:T(8,128)})) %all-reduce.5.cloned.1.call-update) | async-done | bytes 16777232 | tf_op jit(solution)/shard_map/psum | solution.py:173
  1979.3 3.7 fusion.117
  1984.5 48.7 %reduce-scatter.16.cloned.1.call-done = f32[512,256]{1,0:T(8,128)} async-done(((f32[512,2048]{1,0:T(8,128)}), f32[512,256]{1,0:T(8,128)}) %reduce-scatter.16.cloned.1.call-update) | async-done | bytes 524304 | tf_op jit(solution)/shard_map/reduce_scatter | solution.py:251
  2033.2 96.4 %reduce-scatter.14.cloned.1.call-done = f32[256,1536]{1,0:T(8,128)} async-done(((f32[2048,1536]{1,0:T(8,128)}), f32[256,1536]{1,0:T(8,128)}) %reduce-scatter.14.cloned.1.call-update) | async-done | bytes 1572880 | tf_op jit(solution)/shard_map/reduce_scatter | solution.py:250
  2129.7 120.3 %reduce-scatter.18.cloned.1.call-done = f32[256,2048]{1,0:T(8,128)} async-done(((f32[2048,2048]{1,0:T(8,128)}), f32[256,2048]{1,0:T(8,128)}) %reduce-scatter.18.cloned.1.call-update) | async-done | bytes 2097168 | tf_op jit(solution)/shard_map/reduce_scatter | solution.py:252
  2250.0 120.0 %reduce-scatter.20.cloned.1.call-done = f32[2048,256]{1,0:T(8,128)} async-done(((f32[2048,2048]{1,0:T(8,128)}), f32[2048,256]{1,0:T(8,128)}) %reduce-scatter.20.cloned.1.call-update) | async-done | bytes 2097168 | tf_op jit(solution)/shard_map/reduce_scatter | solution.py:253
  (428 shorter events, 214.1 us)
Async XLA Ops:
  7.2 615.3 %copy-start = (bf16[512,2048]{1,0:T(8,128)(2,1)S(1)}, bf16[512,2048]{1,0:T(8,128)(2,1)}, u32[]{:S(2)}) copy-start(bf16[512,2048]{1,0:T(8,128)(2,1)} %param.32) | copy-start | bytes 6291460
  7.2 615.2 %all-gather.2.cloned.1.call-start = ((), (), s32[]{:S(2)}) async-start(), calls=%async_computation.7 | async-start | bytes 10485760 | tf_op jit(solution)/shard_map/all_gather | solution.py:105
  7.2 49.1 %collective-permute-start = (bf16[1,2,256,2048]{3,2,1,0:T(8,128)(2,1)}, bf16[1,2,256,2048]{3,2,1,0:T(8,128)(2,1)}, u32[]{:S(2)}, u32[]{:S(2)}) collective-permute-start(bf16[1,2,256,2048]{3,2,1,0:T(8,128)(2,1)} %bitcast.392), channel_id=1, source_target_pairs={{0,1},{1,0},{2,3},{3,2},{4,5},{5,4},{6,7},{7,6},{8,9},{9,8},{10,11... | collective-permute-start | bytes 6291464 | tf_op jit(solution)/shard_map/ppermute | solution.py:32
  58.9 7.9 copy-start.76
  58.9 7.9 copy-start.77
  58.9 7.9 copy-start.78
  59.0 7.9 copy-start.79
  59.0 7.9 copy-start.80
  59.0 8.5 copy-start.84
  59.0 10.4 copy-start.83
  63.9 317.7 %collective-permute-start.1 = (bf16[2,2,256,2048]{3,2,1,0:T(8,128)(2,1)}, bf16[2,2,256,2048]{3,2,1,0:T(8,128)(2,1)}, u32[]{:S(2)}, u32[]{:S(2)}) collective-permute-start(bf16[2,2,256,2048]{3,2,1,0:T(8,128)(2,1)} %get-tuple-element.558), channel_id=1, source_target_pairs={{0,2},{1,3},{2,0},{3,1},{4,6},{5,7},{6,4},{7,5},{8,10},{9,11},{10,... | collective-permute-start | bytes 12582920 | tf_op jit(solution)/shard_map/ppermute | solution.py:32
  66.7 1137.3 %all-reduce.7.cloned.1.call-start = ((), (), s32[]{:S(2)}) async-start(), calls=%async_computation.16 | async-start | bytes 16777216 | tf_op jit(solution)/shard_map/psum | solution.py:239
  66.8 354.5 %copy-start.50 = (f32[2048]{0:T(1024)}, f32[2048]{0:T(1024)S(1)}, u32[]{:S(2)}) copy-start(f32[2048]{0:T(1024)S(1)} %convert_element_type.264) | copy-start | bytes 24580
  66.9 354.5 %copy-start.52 = (f32[2048]{0:T(1024)}, f32[2048]{0:T(1024)S(1)}, u32[]{:S(2)}) copy-start(f32[2048]{0:T(1024)S(1)} %convert_element_type.265) | copy-start | bytes 24580
  66.9 354.5 %copy-start.58 = (f32[2048]{0:T(1024)}, f32[2048]{0:T(1024)S(1)}, u32[]{:S(2)}) copy-start(f32[2048]{0:T(1024)S(1)} %convert_element_type.270) | copy-start | bytes 24580
  70.7 410.3 %copy-start.41 = (f32[1024,32]{0,1:T(8,128)}, f32[1024,32]{0,1:T(8,128)S(1)}, u32[]{:S(2)}) copy-start(f32[1024,32]{0,1:T(8,128)S(1)} %get-tuple-element.612) | copy-start | bytes 393220
  411.8 5.9 copy-start.6
  420.7 9.8 copy-start.62
  421.3 9.1 copy-start.64
  421.3 9.1 copy-start.66
  421.3 9.1 copy-start.68
  447.6 7.7 copy-start.29
  518.5 15.7 copy-start.8
  557.9 12.6 copy-start.46
  557.9 12.6 copy-start.86
  557.9 15.9 copy-start.28
  557.9 15.9 copy-start.74
  622.4 5.7 copy-start.47
  622.4 5.7 copy-start.87
  637.1 7.3 copy-start.4
  655.9 7.9 copy-start.4
  673.1 7.8 copy-start.9
  673.1 7.8 copy-start.49
  764.5 5.7 copy-start.32
  768.6 9.2 copy-start.42
  780.6 10.9 copy-start.45
  784.5 8.4 copy-start.43
  784.5 8.4 copy-start.44
  807.0 12.1 copy-start.34
  819.1 10.9 copy-start.75
  849.2 14.9 copy-start.92
  864.1 20.3 copy-start.51
  864.1 20.3 copy-start.59
  864.1 20.3 copy-start.63
  864.1 20.3 copy-start.65
  864.1 20.3 copy-start.67
  864.1 20.3 copy-start.69
  912.0 419.1 %reduce-scatter.24.cloned.1.call-start = ((), (), s32[]{:S(2)}) async-start(), calls=%async_computation.13 | async-start | bytes 442368
  914.8 12.9 copy-start.21
  927.7 5.6 copy-start.88
  933.3 13.4 copy-start.60
  933.3 13.4 copy-start.61
  947.7 384.8 %reduce-scatter.26.cloned.1.call-start = ((), (), s32[]{:S(2)}) async-start(), calls=%async_computation.14 | async-start | bytes 1179648
  950.6 467.5 %reduce-scatter.22.cloned.1.call-start = ((), (), s32[]{:S(2)}) async-start(), calls=%async_computation.12 | async-start | bytes 1081344
  1215.5 763.8 %all-reduce.5.cloned.1.call-start = ((), (), s32[]{:S(2)}) async-start(), calls=%async_computation.15 | async-start | bytes 33554432 | tf_op jit(solution)/shard_map/psum | solution.py:173
  1224.8 808.4 %reduce-scatter.16.cloned.1.call-start = ((), (), s32[]{:S(2)}) async-start(), calls=%async_computation.9 | async-start | bytes 4718592 | tf_op jit(solution)/shard_map/reduce_scatter | solution.py:251
  1236.4 893.2 %reduce-scatter.14.cloned.1.call-start = ((), (), s32[]{:S(2)}) async-start(), calls=%async_computation.8 | async-start | bytes 14155776 | tf_op jit(solution)/shard_map/reduce_scatter | solution.py:250
  1242.7 9.6 copy-start.35
  1265.5 984.5 %reduce-scatter.18.cloned.1.call-start = ((), (), s32[]{:S(2)}) async-start(), calls=%async_computation.10 | async-start | bytes 18874368 | tf_op jit(solution)/shard_map/reduce_scatter | solution.py:252
  1265.7 15.6 copy-start.27
  1265.7 15.6 copy-start.91
  1297.3 1072.7 %reduce-scatter.20.cloned.1.call-start = ((), (), s32[]{:S(2)}) async-start(), calls=%async_computation.11 | async-start | bytes 18874368 | tf_op jit(solution)/shard_map/reduce_scatter | solution.py:253
  1297.5 15.5 copy-start.89
  1419.2 950.8 %copy-start.85 = (f32[1,64]{1,0:T(1,128)}, f32[1,64]{1,0:T(1,128)S(1)}, u32[]{:S(2)}) copy-start(f32[1,64]{1,0:T(1,128)S(1)} %copy.162) | copy-start | bytes 772
  (58 other events, 187.8 us)
Sparse Core Ops, SparseCore 0:
  66.8 293.5 all-gather.1
  912.1 291.8 all-reduce.6
  1207.0 32.8 reduce-scatter.23
  1243.0 35.9 reduce-scatter.25
  1281.1 137.0 reduce-scatter.21
  1420.6 558.5 all-reduce.4
  1983.2 49.9 reduce-scatter.15
  2037.3 92.3 reduce-scatter.13
  2133.8 116.1 reduce-scatter.17
  2254.0 115.9 reduce-scatter.19
